TPU v7x, 512 devices: a whole 4x8x8 slice. The times are simulated.
512 devices in a mesh: req: 64 (over x, z, core), mdl: 8 (over y).
Axes of the slice: x: 4, y: 8, z: 8, core: 2. Of those that a mesh axis runs over, the one named last changes fastest.
Arguments:
- queries: bfloat16 [1536, 2048], P('req', 'mdl'), may hold values from -6 to 6
- scored_key_value: bfloat16 [2, 1536, 1024], P(None, 'req', 'mdl'), may hold values from -6 to 6
- gate_logits: bfloat16 [1536, 2048], P('req', 'mdl'), may hold values from -8 to 8
- page_kv: bfloat16 [2, 2176, 128, 1024], P(None, 'req', None, 'mdl'), may hold values from -6 to 6
- page_table: int32 [64, 128], replicated, may hold values from -1 to 2175, as said below
- lengths: int32 [64], replicated, may hold values from 1 to 16384
- assignment: int32 [64], replicated, may hold values from 0 to 63, each once
- offsets: int32 [64, 24], P('req'), may hold values from 0 to 23, each once within a row
- residual: bfloat16 [1536, 2048], P('req'), may hold values from -18 to 18
- out_weight: bfloat16 [2048, 2048], P('mdl'), may hold values from -1 to 1
- norm_gain: bfloat16 [2048], replicated, may hold values from 0.5 to 1.5
- head_weight: bfloat16 [2048, 131072], P(None, ('req', 'mdl')), may hold values from -0.3193592 to 0.3193592
- targets: int32 [1536], replicated, may hold values from 0 to 131071
Outputs:
- logprob: float32 [1536], P('req')
- entropy: float32 [1536], P('req')
Inputs may be any that keep to these rules, and one draw needn't show every extreme that they name: `page_table`: row i lists the pages of request i in order, each as owner index times 34 plus a slot, followed by -1. Request i has ceil(lengths[i] / 128) pages, no page serves two requests, and at most 2 pages of one request sit on one owner. `assignment`: each index along req holds exactly one request. `offsets`: each row is an order of 0 to 23.
All inputs are finite; a program needn't handle non-finite values.
Results may differ from a plain program's by a relative error of at most 0.0013.
Values may be sent and summed in bfloat16 or wider, within the bound.
No kernel may reach another device: no remote copies, remote signals or barrier semaphores. Data moves between devices by JAX's collectives and lax.ppermute only.
A program may use at most 128 MiB of HBM per device.

v0:
```python
import jax
import jax.numpy as jnp
from jax import lax
from jax.sharding import PartitionSpec as P

HEAD_SIZE = 128
CAP = 2


FLOOR_SCORE = -1e30
NORM_EPSILON = 1e-06


def body(
    queries,
    scored_key_value,
    gate_logits,
    page_kv,
    page_table,
    lengths,
    assignment,
    offsets,
    residual,
    out_weight,
    norm_gain,
    head_weight,
    targets,
):
    groups = lax.axis_size("req")
    req_index = lax.axis_index("req")
    fresh_count = queries.shape[0]
    kv_heads = scored_key_value.shape[2] // HEAD_SIZE
    queries_per_group = queries.shape[1] // scored_key_value.shape[2]
    page_len = page_kv.shape[2]
    store_pages = page_kv.shape[1]
    page_slots = page_table.shape[1]
    score_scale = HEAD_SIZE ** (-0.5)
    indices = jnp.arange(groups, dtype=jnp.int32)
    holder = jnp.sum(
        jnp.where(assignment[:, None] == indices[None, :], indices[:, None], 0), axis=0
    )
    query_heads = queries.reshape(fresh_count, kv_heads, queries_per_group, HEAD_SIZE)
    scored_keys = scored_key_value[0].reshape(fresh_count, kv_heads, HEAD_SIZE)
    scored_values = scored_key_value[1].reshape(fresh_count, kv_heads, HEAD_SIZE)
    fresh_order = offsets[0]
    visible = fresh_order[None, :] <= fresh_order[:, None]
    fresh_scores = (
        jnp.einsum("tjgd,ujd->jgtu", query_heads, scored_keys, preferred_element_type=jnp.float32)
        * score_scale
    )
    fresh_scores = jnp.where(visible[None, None], fresh_scores, FLOOR_SCORE)
    fresh_top = jnp.max(fresh_scores, axis=-1)
    page_owner = jnp.where(page_table >= 0, page_table // store_pages, -1)
    page_slot = page_table % store_pages
    is_mine = page_owner == req_index
    page_rank = jnp.cumsum(is_mine.astype(jnp.int32), axis=1) - 1
    slot_picks = [
        jnp.sum(jnp.where(is_mine & (page_rank == cap_index), page_slot, 0), axis=1)
        for cap_index in range(CAP)
    ]
    send_slot = jnp.take(jnp.stack(slot_picks, axis=1), holder, axis=0).reshape(-1)
    outgoing = jnp.take(page_kv, send_slot, axis=1)
    arrived = lax.all_to_all(outgoing, "req", split_axis=1, concat_axis=1, tiled=True)
    request = holder[req_index]
    page_table_row = jnp.take(page_table, request, axis=0)
    length = jnp.take(lengths, request)
    row_owner = jnp.where(page_table_row >= 0, page_table_row // store_pages, -1)
    source = row_owner[None, :] == indices[:, None]
    row_rank = jnp.cumsum(source.astype(jnp.int32), axis=1) - 1
    page_fill = jnp.clip(length - jnp.arange(page_slots, dtype=jnp.int32) * page_len, 0, page_len)
    counts = jnp.stack(
        [
            jnp.sum(jnp.where(source & (row_rank == cap_index), page_fill[None, :], 0), axis=1)
            for cap_index in range(CAP)
        ],
        axis=1,
    ).reshape(-1)
    live_keys = (jnp.arange(page_len, dtype=jnp.int32)[None, :] < counts[:, None]).reshape(-1)
    cached_keys = arrived[0].reshape(-1, kv_heads, HEAD_SIZE)
    cached_values = arrived[1].reshape(-1, kv_heads, HEAD_SIZE)
    scores = (
        jnp.einsum("tjgd,ljd->jgtl", query_heads, cached_keys, preferred_element_type=jnp.float32)
        * score_scale
    )
    scores = jnp.where(live_keys[None, None, None, :], scores, FLOOR_SCORE)
    row_top = jnp.maximum(jnp.max(scores, axis=-1), fresh_top)
    weights = jnp.exp(scores - row_top[..., None])
    weight_sum = jnp.sum(weights, axis=-1)
    summed = jnp.einsum(
        "jgtl,ljd->tjgd",
        weights.astype(jnp.bfloat16),
        cached_values,
        preferred_element_type=jnp.float32,
    )
    fresh_weights = jnp.exp(fresh_scores - row_top[..., None])
    weight_sum = weight_sum + jnp.sum(fresh_weights, axis=-1)
    summed = summed + jnp.einsum(
        "jgtu,ujd->tjgd",
        fresh_weights.astype(jnp.bfloat16),
        scored_values,
        preferred_element_type=jnp.float32,
    )
    attended = summed / jnp.transpose(weight_sum, (2, 0, 1))[..., None]
    gated_out = (
        attended.reshape(fresh_count, -1) * jax.nn.sigmoid(gate_logits.astype(jnp.float32))
    ).astype(jnp.bfloat16)
    update = lax.psum(jnp.dot(gated_out, out_weight, preferred_element_type=jnp.float32), "mdl")
    stream = residual.astype(jnp.float32) + update
    normed = (
        stream
        * lax.rsqrt(jnp.mean(stream * stream, axis=-1, keepdims=True) + NORM_EPSILON)
        * norm_gain.astype(jnp.float32)
    ).astype(jnp.bfloat16)
    logits = jnp.dot(
        lax.all_gather(normed, "req", axis=0, tiled=True),
        head_weight,
        preferred_element_type=jnp.float32,
    )
    vocab_width = head_weight.shape[1]
    vocab_start = (req_index * lax.axis_size("mdl") + lax.axis_index("mdl")) * vocab_width
    columns = vocab_start + jnp.arange(vocab_width, dtype=jnp.int32)
    chosen = jnp.sum(jnp.where(targets[:, None] == columns[None, :], logits, 0.0), axis=1)
    local_peak = jnp.max(logits, axis=1)
    row_peak = lax.pmax(local_peak, ("req", "mdl"))
    vocab_weights = jnp.exp(logits - row_peak[:, None])
    vocab_total, moment, chosen = lax.psum(
        (jnp.sum(vocab_weights, axis=1), jnp.sum(vocab_weights * logits, axis=1), chosen),
        ("req", "mdl"),
    )
    log_total = row_peak + jnp.log(vocab_total)
    logprob = lax.dynamic_slice_in_dim(chosen - log_total, req_index * fresh_count, fresh_count)
    entropy = lax.dynamic_slice_in_dim(
        log_total - moment / vocab_total, req_index * fresh_count, fresh_count
    )
    return (logprob, entropy)


def solution(mesh):
    placed = (
        P("req", "mdl"),
        P(None, "req", "mdl"),
        P("req", "mdl"),
        P(None, "req", None, "mdl"),
        P(),
        P(),
        P(),
        P("req", None),
        P("req", None),
        P("mdl", None),
        P(),
        P(None, ("req", "mdl")),
        P(),
    )
    return jax.shard_map(
        body, mesh=mesh, in_specs=placed, out_specs=(P("req"), P("req")), check_vma=False
    )
```

profile of v0, /device:TPU:1, one launch (start us, length us, event | category | flops | bytes accessed | tf_op | source)
XLA Modules:
  0.0 604.8 jit_solution(16562163437523480842)
XLA Ops:
  7.2 0.9 select_reduce_fusion.5
  8.1 0.8 fusion.49
  8.9 0.3 reduce_window_sum.17
  9.2 0.9 select_reduce_fusion.4
  10.2 0.6 gather_fusion
  10.9 0.1 select_n.156
  11.2 6.4 %gather_fusion.1 = bf16[128,2,128,128]{3,2,1,0:T(8,128)(2,1)} fusion(bf16[2,34,128,128]{3,2,1,0:T(8,128)(2,1)S(1)} %copy-done, s32[1024]{0:T(1024)S(1)} %pad_clamp_fusion), kind=kCustom, calls=%fused_computation.1 | custom fusion | bytes 16777728 | tf_op jit(solution)/shard_map/jit(_take)/gather | solution.py:62
  17.6 7.4 %select_bitcast_fusion = bf16[2,128,128,128]{3,2,0,1:T(8,128)(2,1)} fusion(bf16[128,2,128,128]{3,2,1,0:T(8,128)(2,1)} %gather_fusion.1, pred[128]{0:T(512)(128)(4,1)S(1)} %compare_and_fusion), kind=kLoop, calls=%fused_computation.6 | loop fusion | flops 4194304 | bytes 16777344 | tf_op jit(solution)/shard_map/jit(_take)/select_n | solution.py:62
  25.0 15.2 %all-to-all-start = ((bf16[2,128,128,128]{3,2,0,1:T(8,128)(2,1)}), bf16[2,128,128,128]{3,2,0,1:T(8,128)(2,1)}, u32[]{:S(2)}, u32[]{:S(2)}) async-start(bf16[2,128,128,128]{3,2,0,1:T(8,128)(2,1)} %select_bitcast_fusion), calls=%async_computation | async-start | bytes 16777216 | tf_op jit(solution)/shard_map/all_to_all | solution.py:63
  40.2 0.6 dynamic_slice.9
  42.8 0.6 dynamic-slice.6
  44.0 0.7 bitcast_select_fusion.1
  44.7 0.3 reduce_window_sum.18
  45.3 0.1 lt.95
  45.5 0.2 fusion.52
  45.8 180.1 %all-to-all-done = bf16[2,128,128,128]{3,2,0,1:T(8,128)(2,1)} async-done(((bf16[2,128,128,128]{3,2,0,1:T(8,128)(2,1)}), bf16[2,128,128,128]{3,2,0,1:T(8,128)(2,1)}, u32[]{:S(2)}, u32[]{:S(2)}) %all-to-all-start) | async-done | bytes 8388640 | tf_op jit(solution)/shard_map/all_to_all | solution.py:63
  225.9 4.0 fusion.50
  229.9 2.7 fusion.51
  232.7 0.2 convolution_bitcast_fusion
  232.8 0.7 fusion.3
  233.6 1.0 fusion.16
  234.6 0.2 copy-done.1
  234.8 0.9 fusion.33
  235.8 69.2 %all-reduce.3.cloned.1.call-done = f32[24,2048]{1,0:T(8,128)} async-done(((f32[24,2048]{1,0:T(8,128)}), f32[24,2048]{1,0:T(8,128)}) %all-reduce.3.cloned.1.call-update) | async-done | bytes 196624 | tf_op jit(solution)/shard_map/psum | solution.py:107
  305.0 1.1 multiply_reduce_fusion.1
  306.1 1.6 multiply_convert_fusion
  307.8 91.5 %all-gather.2.cloned.1.call-done = bf16[1536,2048]{1,0:T(8,128)(2,1)} async-done(((bf16[24,2048]{1,0:T(8,128)(2,1)}), bf16[1536,2048]{1,0:T(8,128)(2,1)}) %all-gather.2.cloned.1.call-update) | async-done | bytes 6291472 | tf_op jit(solution)/shard_map/all_gather | solution.py:115
  399.3 5.8 fusion.53
  405.1 95.8 %pmax.7 = f32[1536]{0:T(1024)S(1)} all-reduce(f32[1536]{0:T(1024)S(1)} %get-tuple-element.42), channel_id=1, replica_groups=mesh['req'=64,'mdl'=8] {'req','mdl'}, use_global_device_ids=true, to_apply=%region_16.17 | all-reduce | flops 1536 | bytes 12288 | tf_op jit(solution)/shard_map/pmax | solution.py:124
  501.0 1.9 multiply_reduce_fusion
  502.9 94.5 %all-reduce = (f32[1536]{0:T(1024)S(1)}, f32[1536]{0:T(1024)S(1)}, f32[1536]{0:T(1024)S(1)}) all-reduce(f32[1536]{0:T(1024)S(1)} %get-tuple-element.26, f32[1536]{0:T(1024)S(1)} %get-tuple-element.25, f32[1536]{0:T(1024)S(1)} %get-tuple-element.24), channel_id=1, replica_groups=mesh['req'=64,'mdl'=8] {'req','mdl'}, use_global_device_ids=true, to_apply=%region_14.15 | all-reduce | flops 4608 | bytes 36864 | tf_op jit(solution)/shard_map/psum | solution.py:126
  597.4 0.6 fusion.47
  (49 shorter events, 1.0 us)
Async XLA Ops:
  7.2 4.1 copy-start
  25.0 17.8 %copy-start.10 = (s32[64]{0:T(128)S(1)}, s32[64]{0:T(128)}, u32[]{:S(2)}) copy-start(s32[64]{0:T(128)} %param.18) | copy-start | bytes 772
  25.0 20.4 %copy-start.8 = (s32[1,24]{1,0:T(1,128)S(1)}, s32[1,24]{1,0:T(1,128)}, u32[]{:S(2)}) copy-start(s32[1,24]{1,0:T(1,128)} %param.20) | copy-start | bytes 292
  25.0 20.5 %copy-start.3 = (bf16[24,256]{1,0:T(8,128)(2,1)S(1)}, bf16[24,256]{1,0:T(8,128)(2,1)}, u32[]{:S(2)}) copy-start(bf16[24,256]{1,0:T(8,128)(2,1)} %param.13) | copy-start | bytes 36868
  25.0 20.5 %copy-start.7 = (bf16[2,24,128]{2,1,0:T(8,128)(2,1)S(1)}, bf16[2,24,128]{2,1,0:T(8,128)(2,1)}, u32[]{:S(2)}) copy-start(bf16[2,24,128]{2,1,0:T(8,128)(2,1)} %param.14) | copy-start | bytes 36868
  25.0 200.9 %all-to-all-start = ((bf16[2,128,128,128]{3,2,0,1:T(8,128)(2,1)}), bf16[2,128,128,128]{3,2,0,1:T(8,128)(2,1)}, u32[]{:S(2)}, u32[]{:S(2)}) async-start(bf16[2,128,128,128]{3,2,0,1:T(8,128)(2,1)} %select_bitcast_fusion), calls=%async_computation | async-start | bytes 16777216 | tf_op jit(solution)/shard_map/all_to_all | solution.py:63
  40.2 264.8 %all-reduce.3.cloned.1.call-start = ((), (), s32[]{:S(2)}) async-start(), calls=%async_computation.1 | async-start | bytes 393216 | tf_op jit(solution)/shard_map/psum | solution.py:107
  233.6 1.2 copy-start.1
  233.6 1.2 copy-start.4
  233.6 2.2 copy-start.6
  233.6 71.4 %copy-start.2 = (bf16[24,2048]{1,0:T(8,128)(2,1)S(1)}, bf16[24,2048]{1,0:T(8,128)(2,1)}, u32[]{:S(2)}) copy-start(bf16[24,2048]{1,0:T(8,128)(2,1)} %param.21) | copy-start | bytes 294916
  233.6 165.7 %copy-start.9 = (bf16[2048,256]{1,0:T(8,128)(2,1)S(1)}, bf16[2048,256]{1,0:T(8,128)(2,1)}, u32[]{:S(2)}) copy-start(bf16[2048,256]{1,0:T(8,128)(2,1)} %param.24) | copy-start | bytes 3145732
  235.8 163.6 %all-gather.2.cloned.1.call-start = ((), (), s32[]{:S(2)}) async-start(), calls=%async_computation.2 | async-start | bytes 6389760 | tf_op jit(solution)/shard_map/all_gather | solution.py:115
  307.8 193.2 %copy-start.5 = (s32[1536]{0:T(1024)S(1)}, s32[1536]{0:T(1024)}, u32[]{:S(2)}) copy-start(s32[1536]{0:T(1024)} %param.25) | copy-start | bytes 18436
Sparse Core Ops, SparseCore 0:
  235.9 69.0 all-reduce.2
  308.3 90.9 all-gather.1
where the time goes:
time: 605 us
  waiting for transfers between devices  341 us (56%)
  blocking collectives  190 us (31%)
  other arithmetic  17.7 us (3%)
  between operations  16.9 us (3%)
  starting transfers between devices  15.2 us (3%)
  local copies, waits for them, and re-layouts  13 us (2%)
  matrix products  10.7 us (2%)
    all_to_all x1, waiting for transfers between devices, body(): lax.all_to_all(outgoing, 'req', split_axis=1, concat_axis=1, tiled=True)  180 us
    pmax x1, blocking collectives, body(): row_peak = lax.pmax(local_peak, ('req', 'mdl'))  95.8 us
    psum x1, blocking collectives, body(): lax.psum((jnp.sum(vocab_weights, axis=1), jnp.sum(vocab_weights * logits,...  94.5 us
    all_gather x1, waiting for transfers between devices, body(): lax.all_gather(normed, 'req', axis=0, tiled=True)  91.5 us
    psum x1, waiting for transfers between devices, body(): lax.psum(jnp.dot(gated_out, out_weight, preferred_element_type=jnp.float3...  69.2 us
    all_to_all x1, starting transfers between devices, body(): lax.all_to_all(outgoing, 'req', split_axis=1, concat_axis=1, tiled=True)  15.2 us
  transfers between devices with their start and end apart: 3, of which 3 were waited for; matrix products, arithmetic and copies ran while one was open for 0% of the time, Pallas kernels for 0%

commit v1 on v0

--- a/solution.py
+++ b/solution.py
@@ -9,6 +9,15 @@
 
 FLOOR_SCORE = -1e30
 NORM_EPSILON = 1e-06
+
+
+def merge_stats(parts):
+    peak = jnp.max(parts[:, :, 0], axis=0)
+    scale = jnp.exp(parts[:, :, 0] - peak[None])
+    total = jnp.sum(parts[:, :, 1] * scale, axis=0)
+    moment = jnp.sum(parts[:, :, 2] * scale, axis=0)
+    chosen = jnp.sum(parts[:, :, 3], axis=0)
+    return jnp.stack([peak, total, moment, chosen], axis=1)
 
 
 def body(
@@ -117,21 +126,32 @@
         preferred_element_type=jnp.float32,
     )
     vocab_width = head_weight.shape[1]
-    vocab_start = (req_index * lax.axis_size("mdl") + lax.axis_index("mdl")) * vocab_width
+    mdl_size = lax.axis_size("mdl")
+    mdl_index = lax.axis_index("mdl")
+    vocab_start = (req_index * mdl_size + mdl_index) * vocab_width
     columns = vocab_start + jnp.arange(vocab_width, dtype=jnp.int32)
     chosen = jnp.sum(jnp.where(targets[:, None] == columns[None, :], logits, 0.0), axis=1)
     local_peak = jnp.max(logits, axis=1)
-    row_peak = lax.pmax(local_peak, ("req", "mdl"))
-    vocab_weights = jnp.exp(logits - row_peak[:, None])
-    vocab_total, moment, chosen = lax.psum(
-        (jnp.sum(vocab_weights, axis=1), jnp.sum(vocab_weights * logits, axis=1), chosen),
-        ("req", "mdl"),
+    local_weights = jnp.exp(logits - local_peak[:, None])
+    stats = jnp.stack(
+        [
+            local_peak,
+            jnp.sum(local_weights, axis=1),
+            jnp.sum(local_weights * logits, axis=1),
+            chosen,
+        ],
+        axis=1,
+    ).reshape(groups, fresh_count, 4)
+    stats = lax.all_to_all(stats, "req", 0, 0, tiled=True)
+    stats = merge_stats(stats)
+    slots = jnp.where(
+        (jnp.arange(mdl_size, dtype=jnp.int32) == mdl_index)[:, None, None], stats[None], 0.0
     )
+    stats = merge_stats(lax.psum(slots, "mdl"))
+    row_peak, vocab_total, moment, chosen = (stats[:, i] for i in range(4))
     log_total = row_peak + jnp.log(vocab_total)
-    logprob = lax.dynamic_slice_in_dim(chosen - log_total, req_index * fresh_count, fresh_count)
-    entropy = lax.dynamic_slice_in_dim(
-        log_total - moment / vocab_total, req_index * fresh_count, fresh_count
-    )
+    logprob = chosen - log_total
+    entropy = log_total - moment / vocab_total
     return (logprob, entropy)
 
 

time: 605 us -> 461 us (0.76)
  blocking collectives: 190 us -> 22.5 us
  waiting for transfers between devices: 341 us -> 351 us
    pmax x1 -> x0, blocking collectives: 95.8 us -> none  [body(): row_peak = lax.pmax(local_peak, ('req', 'mdl'))]
    psum x1, blocking collectives: 94.5 us -> 22.5 us  [body(): stats = merge_stats(lax.psum(slots, 'mdl'))]
    all_to_all x0 -> x1, waiting for transfers between devices: none -> 10.3 us  [body(): stats = lax.all_to_all(stats, 'req', 0, 0, tiled=True)]
  transfers between devices with their start and end apart: 3 -> 4, of which waited for: 3 -> 4; matrix products, arithmetic and copies ran while one was open for 0% -> 1% of each run, Pallas kernels for 0% -> 0%
where the time goes in v1:
time: 461 us; the launch traced here: 455 us
  waiting for transfers between devices  351 us (76%)
  blocking collectives  22.5 us (5%)
  starting transfers between devices  21.2 us (5%)
  other arithmetic  18.1 us (4%)
  between operations  16.9 us (4%)
  local copies, waits for them, and re-layouts  14.2 us (3%)
  matrix products  10.7 us (2%)
    all_to_all x1, waiting for transfers between devices, body(): lax.all_to_all(outgoing, 'req', split_axis=1, concat_axis=1, tiled=True)  180 us
    all_gather x1, waiting for transfers between devices, body(): lax.all_gather(normed, 'req', axis=0, tiled=True)  91.5 us
    psum x1, waiting for transfers between devices, body(): lax.psum(jnp.dot(gated_out, out_weight, preferred_element_type=jnp.float3...  69.1 us
    psum x1, blocking collectives, body(): stats = merge_stats(lax.psum(slots, 'mdl'))  22.5 us
    all_to_all x1, starting transfers between devices, body(): lax.all_to_all(outgoing, 'req', split_axis=1, concat_axis=1, tiled=True)  15.2 us
    all_to_all x1, waiting for transfers between devices, body(): stats = lax.all_to_all(stats, 'req', 0, 0, tiled=True)  10.3 us
  transfers between devices with their start and end apart: 4, of which 4 were waited for; matrix products, arithmetic and copies ran while one was open for 1% of the time, Pallas kernels for 0%

profile of v1, /device:TPU:1, one launch (start us, length us, event | category | flops | bytes accessed | tf_op | source)
XLA Modules:
  0.0 454.9 jit_solution(17138256541954221748)
XLA Ops:
  7.2 0.9 select_reduce_fusion.5
  8.1 0.8 fusion.57
  8.9 0.3 reduce_window_sum.17
  9.2 0.9 select_reduce_fusion.4
  10.2 0.6 gather_fusion
  11.2 6.3 %gather_fusion.1 = bf16[128,2,128,128]{3,2,1,0:T(8,128)(2,1)} fusion(bf16[2,34,128,128]{3,2,1,0:T(8,128)(2,1)S(1)} %copy-done, s32[1024]{0:T(1024)S(1)} %pad_clamp_fusion), kind=kCustom, calls=%fused_computation.1 | custom fusion | bytes 16777728 | tf_op jit(solution)/shard_map/jit(_take)/gather | solution.py:71
  17.6 7.4 %select_bitcast_fusion = bf16[2,128,128,128]{3,2,0,1:T(8,128)(2,1)} fusion(bf16[128,2,128,128]{3,2,1,0:T(8,128)(2,1)} %gather_fusion.1, pred[128]{0:T(512)(128)(4,1)S(1)} %compare_and_fusion), kind=kLoop, calls=%fused_computation.6 | loop fusion | flops 4194304 | bytes 16777344 | tf_op jit(solution)/shard_map/jit(_take)/select_n | solution.py:71
  25.0 15.2 %all-to-all-start = ((bf16[2,128,128,128]{3,2,0,1:T(8,128)(2,1)}), bf16[2,128,128,128]{3,2,0,1:T(8,128)(2,1)}, u32[]{:S(2)}, u32[]{:S(2)}) async-start(bf16[2,128,128,128]{3,2,0,1:T(8,128)(2,1)} %select_bitcast_fusion), calls=%async_computation | async-start | bytes 16777216 | tf_op jit(solution)/shard_map/all_to_all | solution.py:72
  40.2 0.6 dynamic_slice.3
  42.8 0.6 dynamic-slice.6
  44.0 0.7 bitcast_select_fusion.1
  44.7 0.3 reduce_window_sum.18
  45.8 180.1 %all-to-all-done = bf16[2,128,128,128]{3,2,0,1:T(8,128)(2,1)} async-done(((bf16[2,128,128,128]{3,2,0,1:T(8,128)(2,1)}), bf16[2,128,128,128]{3,2,0,1:T(8,128)(2,1)}, u32[]{:S(2)}, u32[]{:S(2)}) %all-to-all-start) | async-done | bytes 8388640 | tf_op jit(solution)/shard_map/all_to_all | solution.py:72
  225.9 4.0 fusion.58
  229.9 2.7 fusion.60
  232.7 0.2 convolution_bitcast_fusion
  232.8 0.7 fusion.3
  233.6 1.0 fusion.16
  234.6 0.2 copy-done.1
  234.8 0.9 fusion.33
  235.8 69.1 %all-reduce.2.cloned.1.call-done = f32[24,2048]{1,0:T(8,128)} async-done(((f32[24,2048]{1,0:T(8,128)}), f32[24,2048]{1,0:T(8,128)}) %all-reduce.2.cloned.1.call-update) | async-done | bytes 196624 | tf_op jit(solution)/shard_map/psum | solution.py:116
  305.0 1.1 multiply_reduce_fusion.1
  306.0 1.6 multiply_convert_fusion
  307.8 91.5 %all-gather.2.cloned.1.call-done = bf16[1536,2048]{1,0:T(8,128)(2,1)} async-done(((bf16[24,2048]{1,0:T(8,128)(2,1)}), bf16[1536,2048]{1,0:T(8,128)(2,1)}) %all-gather.2.cloned.1.call-update) | async-done | bytes 6291472 | tf_op jit(solution)/shard_map/all_gather | solution.py:124
  399.3 5.8 %fusion.62 = (f32[1536]{0:T(1024)S(1)}, f32[1536,256]{0,1:T(8,128)}) fusion(bf16[1536,2048]{1,0:T(8,128)(2,1)} %all-gather.2.cloned.1.call-done, bf16[2048,256]{1,0:T(8,128)(2,1)S(1)} %copy-done.9), kind=kOutput, calls=%fused_computation.115 | convolution fusion | flops 1611004416 | bytes 8919040 | tf_op jit(solution)/shard_map/dot_general | solution.py:123
  405.2 1.9 fusion.8
  407.3 0.7 copy.55
  408.1 5.9 %all-to-all-start.1 = ((f32[64,24,4]{1,2,0:T(4,128)}), f32[64,24,4]{1,2,0:T(4,128)S(1)}, u32[]{:S(2)}, u32[]{:S(2)}) async-start(f32[64,24,4]{1,2,0:T(4,128)} %copy.55), calls=%async_computation.1 | async-start | bytes 262144 | tf_op jit(solution)/shard_map/all_to_all | solution.py:145
  414.0 10.3 %all-to-all-done.1 = f32[64,24,4]{1,2,0:T(4,128)S(1)} async-done(((f32[64,24,4]{1,2,0:T(4,128)}), f32[64,24,4]{1,2,0:T(4,128)S(1)}, u32[]{:S(2)}, u32[]{:S(2)}) %all-to-all-start.1) | async-done | bytes 24608 | tf_op jit(solution)/shard_map/all_to_all | solution.py:145
  424.6 0.2 fusion.39
  425.0 22.5 %psum.15 = f32[8,24,4]{1,0,2:T(8,128)S(1)} all-reduce(f32[8,24,4]{1,0,2:T(8,128)S(1)} %broadcast_select_fusion.1), channel_id=1, replica_groups=mesh['req'=64,'mdl'=8] {'mdl'}, use_global_device_ids=true, to_apply=%region_21.22 | all-reduce | flops 768 | bytes 6144 | tf_op jit(solution)/shard_map/psum | solution.py:150
  447.5 0.5 divide_subtract_fusion
  (65 shorter events, 2.3 us)
Async XLA Ops:
  7.2 4.1 copy-start
  25.0 17.8 %copy-start.10 = (s32[64]{0:T(128)S(1)}, s32[64]{0:T(128)}, u32[]{:S(2)}) copy-start(s32[64]{0:T(128)} %param.18) | copy-start | bytes 772
  25.0 20.4 %copy-start.8 = (s32[1,24]{1,0:T(1,128)S(1)}, s32[1,24]{1,0:T(1,128)}, u32[]{:S(2)}) copy-start(s32[1,24]{1,0:T(1,128)} %param.20) | copy-start | bytes 292
  25.0 20.5 %copy-start.3 = (bf16[24,256]{1,0:T(8,128)(2,1)S(1)}, bf16[24,256]{1,0:T(8,128)(2,1)}, u32[]{:S(2)}) copy-start(bf16[24,256]{1,0:T(8,128)(2,1)} %param.13) | copy-start | bytes 36868
  25.0 20.5 %copy-start.7 = (bf16[2,24,128]{2,1,0:T(8,128)(2,1)S(1)}, bf16[2,24,128]{2,1,0:T(8,128)(2,1)}, u32[]{:S(2)}) copy-start(bf16[2,24,128]{2,1,0:T(8,128)(2,1)} %param.14) | copy-start | bytes 36868
  25.0 200.9 %all-to-all-start = ((bf16[2,128,128,128]{3,2,0,1:T(8,128)(2,1)}), bf16[2,128,128,128]{3,2,0,1:T(8,128)(2,1)}, u32[]{:S(2)}, u32[]{:S(2)}) async-start(bf16[2,128,128,128]{3,2,0,1:T(8,128)(2,1)} %select_bitcast_fusion), calls=%async_computation | async-start | bytes 16777216 | tf_op jit(solution)/shard_map/all_to_all | solution.py:72
  40.2 264.8 %all-reduce.2.cloned.1.call-start = ((), (), s32[]{:S(2)}) async-start(), calls=%async_computation.2 | async-start | bytes 393216 | tf_op jit(solution)/shard_map/psum | solution.py:116
  233.6 1.2 copy-start.1
  233.6 1.2 copy-start.4
  233.6 2.2 copy-start.6
  233.6 71.4 %copy-start.2 = (bf16[24,2048]{1,0:T(8,128)(2,1)S(1)}, bf16[24,2048]{1,0:T(8,128)(2,1)}, u32[]{:S(2)}) copy-start(bf16[24,2048]{1,0:T(8,128)(2,1)} %param.21) | copy-start | bytes 294916
  233.6 165.7 %copy-start.9 = (bf16[2048,256]{1,0:T(8,128)(2,1)S(1)}, bf16[2048,256]{1,0:T(8,128)(2,1)}, u32[]{:S(2)}) copy-start(bf16[2048,256]{1,0:T(8,128)(2,1)} %param.24) | copy-start | bytes 3145732
  235.8 163.5 %all-gather.2.cloned.1.call-start = ((), (), s32[]{:S(2)}) async-start(), calls=%async_computation.3 | async-start | bytes 6389760 | tf_op jit(solution)/shard_map/all_gather | solution.py:124
  307.7 97.4 %copy-start.5 = (s32[1536]{0:T(1024)S(1)}, s32[1536]{0:T(1024)}, u32[]{:S(2)}) copy-start(s32[1536]{0:T(1024)} %param.25) | copy-start | bytes 18436
  408.1 16.2 %all-to-all-start.1 = ((f32[64,24,4]{1,2,0:T(4,128)}), f32[64,24,4]{1,2,0:T(4,128)S(1)}, u32[]{:S(2)}, u32[]{:S(2)}) async-start(f32[64,24,4]{1,2,0:T(4,128)} %copy.55), calls=%async_computation.1 | async-start | bytes 262144 | tf_op jit(solution)/shard_map/all_to_all | solution.py:145
Sparse Core Ops, SparseCore 0:
  235.9 69.0 all-reduce.1
  308.3 90.9 all-gather.1

commit v2 on v1

--- a/solution.py
+++ b/solution.py
@@ -59,74 +59,115 @@
     )
     fresh_scores = jnp.where(visible[None, None], fresh_scores, FLOOR_SCORE)
     fresh_top = jnp.max(fresh_scores, axis=-1)
+    fresh_weights = jnp.exp(fresh_scores - fresh_top[..., None])
+    fresh_sum = jnp.sum(fresh_weights, axis=-1)
+    fresh_acc = jnp.einsum(
+        "jgtu,ujd->jgtd",
+        fresh_weights.astype(jnp.bfloat16),
+        scored_values,
+        preferred_element_type=jnp.float32,
+    )
+    all_queries = lax.all_to_all(
+        jnp.broadcast_to(query_heads[None], (groups,) + query_heads.shape), "req", 0, 0, tiled=True
+    )
     page_owner = jnp.where(page_table >= 0, page_table // store_pages, -1)
     page_slot = page_table % store_pages
     is_mine = page_owner == req_index
     page_rank = jnp.cumsum(is_mine.astype(jnp.int32), axis=1) - 1
+    page_fill = jnp.clip(
+        lengths[:, None] - jnp.arange(page_slots, dtype=jnp.int32)[None, :] * page_len, 0, page_len
+    )
     slot_picks = [
         jnp.sum(jnp.where(is_mine & (page_rank == cap_index), page_slot, 0), axis=1)
         for cap_index in range(CAP)
     ]
+    fill_picks = [
+        jnp.sum(jnp.where(is_mine & (page_rank == cap_index), page_fill, 0), axis=1)
+        for cap_index in range(CAP)
+    ]
     send_slot = jnp.take(jnp.stack(slot_picks, axis=1), holder, axis=0).reshape(-1)
-    outgoing = jnp.take(page_kv, send_slot, axis=1)
-    arrived = lax.all_to_all(outgoing, "req", split_axis=1, concat_axis=1, tiled=True)
-    request = holder[req_index]
-    page_table_row = jnp.take(page_table, request, axis=0)
-    length = jnp.take(lengths, request)
-    row_owner = jnp.where(page_table_row >= 0, page_table_row // store_pages, -1)
-    source = row_owner[None, :] == indices[:, None]
-    row_rank = jnp.cumsum(source.astype(jnp.int32), axis=1) - 1
-    page_fill = jnp.clip(length - jnp.arange(page_slots, dtype=jnp.int32) * page_len, 0, page_len)
-    counts = jnp.stack(
-        [
-            jnp.sum(jnp.where(source & (row_rank == cap_index), page_fill[None, :], 0), axis=1)
-            for cap_index in range(CAP)
-        ],
-        axis=1,
-    ).reshape(-1)
-    live_keys = (jnp.arange(page_len, dtype=jnp.int32)[None, :] < counts[:, None]).reshape(-1)
-    cached_keys = arrived[0].reshape(-1, kv_heads, HEAD_SIZE)
-    cached_values = arrived[1].reshape(-1, kv_heads, HEAD_SIZE)
+    send_fill = jnp.take(jnp.stack(fill_picks, axis=1), holder, axis=0)
+    outgoing = jnp.take(page_kv, send_slot, axis=1, mode="clip").reshape(
+        2, groups, CAP * page_len, kv_heads, HEAD_SIZE
+    )
+    live_keys = (
+        jnp.arange(page_len, dtype=jnp.int32)[None, None, :] < send_fill[:, :, None]
+    ).reshape(groups, CAP * page_len)
     scores = (
-        jnp.einsum("tjgd,ljd->jgtl", query_heads, cached_keys, preferred_element_type=jnp.float32)
+        jnp.einsum(
+            "btjgd,bljd->bjgtl", all_queries, outgoing[0], preferred_element_type=jnp.float32
+        )
         * score_scale
     )
-    scores = jnp.where(live_keys[None, None, None, :], scores, FLOOR_SCORE)
-    row_top = jnp.maximum(jnp.max(scores, axis=-1), fresh_top)
-    weights = jnp.exp(scores - row_top[..., None])
-    weight_sum = jnp.sum(weights, axis=-1)
-    summed = jnp.einsum(
-        "jgtl,ljd->tjgd",
+    live = live_keys[:, None, None, None, :]
+    scores = jnp.where(live, scores, FLOOR_SCORE)
+    part_top = lax.reduce_precision(jnp.max(scores, axis=-1), exponent_bits=8, mantissa_bits=7)
+    weights = jnp.where(live, jnp.exp(scores - part_top[..., None]), 0.0)
+    part_sum = jnp.sum(weights, axis=-1)
+    part_acc = jnp.einsum(
+        "bjgtl,bljd->bjgtd",
         weights.astype(jnp.bfloat16),
-        cached_values,
+        outgoing[1],
         preferred_element_type=jnp.float32,
     )
-    fresh_weights = jnp.exp(fresh_scores - row_top[..., None])
-    weight_sum = weight_sum + jnp.sum(fresh_weights, axis=-1)
-    summed = summed + jnp.einsum(
-        "jgtu,ujd->tjgd",
-        fresh_weights.astype(jnp.bfloat16),
-        scored_values,
-        preferred_element_type=jnp.float32,
-    )
-    attended = summed / jnp.transpose(weight_sum, (2, 0, 1))[..., None]
+    sum_high = lax.reduce_precision(part_sum, exponent_bits=8, mantissa_bits=7)
+    sum_rest = part_sum - sum_high
+    sum_mid = lax.reduce_precision(sum_rest, exponent_bits=8, mantissa_bits=7)
+    sum_low = sum_rest - sum_mid
+    lanes = part_acc.shape[-1]
+    pad = ((0, 0),) * 3 + ((0, lanes - fresh_count),)
+    payload = jnp.concatenate(
+        [part_acc]
+        + [jnp.pad(v, pad)[..., None, :] for v in (part_top, sum_high, sum_mid, sum_low)],
+        axis=3,
+    ).astype(jnp.bfloat16)
+    arrived = lax.all_to_all(payload, "req", 0, 0, tiled=True).astype(jnp.float32)
+    arrived_acc = arrived[:, :, :, :fresh_count, :]
+    arrived_top = arrived[:, :, :, fresh_count, :fresh_count]
+    arrived_sum = (
+        arrived[:, :, :, fresh_count + 1, :fresh_count]
+        + arrived[:, :, :, fresh_count + 2, :fresh_count]
+    ) + arrived[:, :, :, fresh_count + 3, :fresh_count]
+    row_top = jnp.maximum(jnp.max(arrived_top, axis=0), fresh_top)
+    arrived_scale = jnp.exp(arrived_top - row_top[None])
+    fresh_scale = jnp.exp(fresh_top - row_top)
+    weight_sum = jnp.sum(arrived_sum * arrived_scale, axis=0) + fresh_sum * fresh_scale
+    summed = (
+        jnp.sum(arrived_acc * arrived_scale[..., None], axis=0)
+        + fresh_acc * fresh_scale[..., None]
+    )
+    attended = jnp.transpose(summed / weight_sum[..., None], (2, 0, 1, 3))
     gated_out = (
         attended.reshape(fresh_count, -1) * jax.nn.sigmoid(gate_logits.astype(jnp.float32))
     ).astype(jnp.bfloat16)
-    update = lax.psum(jnp.dot(gated_out, out_weight, preferred_element_type=jnp.float32), "mdl")
-    stream = residual.astype(jnp.float32) + update
-    normed = (
+    update = jnp.dot(gated_out, out_weight, preferred_element_type=jnp.float32)
+    mdl_size = lax.axis_size("mdl")
+    mdl_index = lax.axis_index("mdl")
+    share = fresh_count // mdl_size
+    terms = lax.all_to_all(
+        update.reshape(mdl_size, share, update.shape[1]), "mdl", 0, 0, tiled=True
+    )
+    row_update = terms[0]
+    for member in range(1, mdl_size):
+        row_update = row_update + terms[member]
+    stream = (
+        lax.dynamic_slice_in_dim(residual, mdl_index * share, share, 0).astype(jnp.float32)
+        + row_update
+    )
+    normed_rows = (
         stream
         * lax.rsqrt(jnp.mean(stream * stream, axis=-1, keepdims=True) + NORM_EPSILON)
         * norm_gain.astype(jnp.float32)
     ).astype(jnp.bfloat16)
+    normed = lax.all_to_all(
+        jnp.broadcast_to(normed_rows[None], (mdl_size,) + normed_rows.shape), "mdl", 0, 0, tiled=True
+    ).reshape(fresh_count, normed_rows.shape[1])
     logits = jnp.dot(
         lax.all_gather(normed, "req", axis=0, tiled=True),
         head_weight,
         preferred_element_type=jnp.float32,
     )
     vocab_width = head_weight.shape[1]
-    mdl_size = lax.axis_size("mdl")
     mdl_index = lax.axis_index("mdl")
     vocab_start = (req_index * mdl_size + mdl_index) * vocab_width
     columns = vocab_start + jnp.arange(vocab_width, dtype=jnp.int32)
@@ -144,10 +185,9 @@
     ).reshape(groups, fresh_count, 4)
     stats = lax.all_to_all(stats, "req", 0, 0, tiled=True)
     stats = merge_stats(stats)
-    slots = jnp.where(
-        (jnp.arange(mdl_size, dtype=jnp.int32) == mdl_index)[:, None, None], stats[None], 0.0
-    )
-    stats = merge_stats(lax.psum(slots, "mdl"))
+    stats = merge_stats(
+        lax.all_to_all(jnp.broadcast_to(stats[None], (mdl_size,) + stats.shape), "mdl", 0, 0, tiled=True)
+    )
     row_peak, vocab_total, moment, chosen = (stats[:, i] for i in range(4))
     log_total = row_peak + jnp.log(vocab_total)
     logprob = chosen - log_total

time: 461 us -> 264 us (0.57); the launches traced: 455 us -> 263 us
  waiting for transfers between devices: 351 us -> 124 us
  blocking collectives: 22.5 us -> 39.1 us
  local copies, waits for them, and re-layouts: 14.2 us -> 26.8 us
  matrix products: 10.7 us -> 17.8 us
  starting transfers between devices: 21.2 us -> 28.1 us
  other arithmetic: 18.1 us -> 12.9 us
    all_to_all x2 -> x3, waiting for transfers between devices: 190 us -> 42.6 us  [the longest x1 25.4 us: body(): lax.all_to_all(payload, 'req', 0, 0, tiled=True).astype(jnp.float32)]
    psum x1 -> x0, waiting for transfers between devices: 69.1 us -> none  [body(): lax.psum(jnp.dot(gated_out, out_weight, preferred_element_type=jnp.float3...]
    all_to_all x0 -> x3, blocking collectives: none -> 39.1 us  [the longest x1 16 us: body(): stats = lax.all_to_all(stats, 'req', 0, 0, tiled=True)]
    psum x1 -> x0, blocking collectives: 22.5 us -> none  [body(): stats = merge_stats(lax.psum(slots, 'mdl'))]
    all_gather x1, waiting for transfers between devices: 91.5 us -> 81 us  [body(): lax.all_gather(normed, 'req', axis=0, tiled=True)]
    select_n x6 -> x2, other arithmetic: 8.27 us -> 0.08 us  [body(): send_fill = jnp.take(jnp.stack(fill_picks, axis=1), holder, axis=0)]
    dot_general x4, matrix products: 4.76 us -> 11.6 us  [the longest x1 5.05 us: body(): jnp.einsum('bjgtl,bljd->bjgtd', weights.astype(jnp.bfloat16), outgoing[1]...]
    all_to_all x2 -> x3, starting transfers between devices: 21.1 us -> 27.9 us  [the longest x1 14.8 us: body(): lax.all_to_all(jnp.broadcast_to(query_heads[None], (groups,) + query_head...]
  transfers between devices with their start and end apart: 4 -> 4, of which waited for: 4 -> 4; matrix products, arithmetic and copies ran while one was open for 1% -> 7% of each run, Pallas kernels for 0% -> 0%
where the time goes in v2:
time: 264 us; the launch traced here: 263 us
  waiting for transfers between devices  124 us (47%)
  blocking collectives  39.1 us (15%)
  starting transfers between devices  28.1 us (11%)
  local copies, waits for them, and re-layouts  26.8 us (10%)
  matrix products  17.8 us (7%)
  between operations  14.5 us (5%)
  other arithmetic  12.9 us (5%)
    all_gather x1, waiting for transfers between devices, body(): lax.all_gather(normed, 'req', axis=0, tiled=True)  81 us
    all_to_all x1, waiting for transfers between devices, body(): lax.all_to_all(payload, 'req', 0, 0, tiled=True).astype(jnp.float32)  25.4 us
    all_to_all x1, blocking collectives, body(): stats = lax.all_to_all(stats, 'req', 0, 0, tiled=True)  16 us
    all_to_all x1, starting transfers between devices, body(): lax.all_to_all(jnp.broadcast_to(query_heads[None], (groups,) + query_head...  14.8 us
    all_to_all x1, blocking collectives, body(): lax.all_to_all(jnp.broadcast_to(stats[None], (mdl_size,) + stats.shape),...  12.9 us
    all_to_all x1, waiting for transfers between devices, body(): lax.all_to_all(update.reshape(mdl_size, share, update.shape[1]), 'mdl', 0...  11.5 us
    all_to_all x1, blocking collectives, body(): lax.all_to_all(jnp.broadcast_to(normed_rows[None], (mdl_size,) + normed_r...  10.1 us
    all_to_all x1, starting transfers between devices, body(): lax.all_to_all(update.reshape(mdl_size, share, update.shape[1]), 'mdl', 0...  6.82 us
  transfers between devices with their start and end apart: 4, of which 4 were waited for; matrix products, arithmetic and copies ran while one was open for 7% of the time, Pallas kernels for 0%

profile of v2, /device:TPU:1, one launch (start us, length us, event | category | flops | bytes accessed | tf_op | source)
XLA Modules:
  0.0 262.7 jit_solution(3485152641139055879)
XLA Ops:
  7.2 0.9 copy_bitcast_fusion
  8.0 1.0 broadcast_in_dim.117
  9.0 14.8 %all-to-all-start = ((bf16[64,24,1,2,128]{4,1,3,2,0:T(8,128)(2,1)}), bf16[64,24,1,2,128]{4,1,3,2,0:T(8,128)(2,1)S(1)}, u32[]{:S(2)}, u32[]{:S(2)}) async-start(bf16[64,24,1,2,128]{4,1,3,2,0:T(8,128)(2,1)} %broadcast_in_dim.117), calls=%async_computation | async-start | bytes 1572864 | tf_op jit(solution)/shard_map/all_to_all | solution.py:70
  23.9 0.8 fusion.61
  25.0 1.0 select_reduce_fusion.2
  26.1 0.8 select_reduce_fusion.3
  28.4 6.4 %gather_fusion = bf16[128,2,128,128]{3,2,1,0:T(8,128)(2,1)} fusion(bf16[2,34,128,128]{3,2,1,0:T(8,128)(2,1)S(1)} %copy-done, s32[1024]{0:T(1024)S(1)} %pad_clamp_fusion), kind=kCustom, calls=%fused_computation.2 | custom fusion | bytes 16777728 | tf_op jit(solution)/shard_map/jit(_take)/gather | solution.py:90
  34.9 6.1 %fusion.63 = (bf16[1,128,128,128]{3,2,0,1:T(8,128)(2,1)}, bf16[1,128,128,128]{3,2,0,1:T(8,128)(2,1)}) fusion(bf16[2,128,128,128]{3,2,0,1:T(8,128)(2,1)} %bitcast.190), kind=kLoop, calls=%fused_computation.134 | loop fusion | bytes 16777216 | tf_op jit(solution)/shard_map/slice | solution.py:98
  41.0 5.8 %all-to-all-done = bf16[64,24,1,2,128]{4,1,3,2,0:T(8,128)(2,1)S(1)} async-done(((bf16[64,24,1,2,128]{4,1,3,2,0:T(8,128)(2,1)}), bf16[64,24,1,2,128]{4,1,3,2,0:T(8,128)(2,1)S(1)}, u32[]{:S(2)}, u32[]{:S(2)}) %all-to-all-start) | async-done | bytes 786464 | tf_op jit(solution)/shard_map/all_to_all | solution.py:70
  46.8 4.9 %bitcast_reduce_fusion = (f32[64,2,24]{2,1,0:T(2,128)S(1)}, f32[64,256,24,2]{1,2,3,0:T(8,128)S(1)}) fusion(pred[64,256]{1,0:T(8,128)(4,1)S(1)} %bitcast_compare_fusion, bf16[64,256,128,1]{2,1,3,0:T(8,128)(2,1)} %bitcast.191, bf16[64,24,1,2,128]{4,1,3,2,0:T(8,128)(2,1)S(1)} %all-to-all-done), kind=kOutput, calls=%fused_computation.4 | convolution fusion | flops 203682816 | bytes 8155136 | tf_op jit(solution)/shard_map/btjgd,bljd->bjgtl/dot_general | solution.py:97
  51.8 1.6 copy-done.1
  53.4 1.4 fusion.2
  55.3 5.0 %fusion.18 = bf16[64,1,2,24,128]{4,3,2,0,1:T(8,128)(2,1)} fusion(bf16[64,256,128,1]{2,1,3,0:T(8,128)(2,1)} %bitcast.192, f32[64,256,24,2]{1,2,3,0:T(8,128)} %copy-done.1, f32[64,2,24]{2,1,0:T(2,128)S(1)} %get-tuple-element.30, pred[64,256]{1,0:T(8,128)(4,1)S(1)} %bitcast_compare_fusion), kind=kOutput, calls=%fused_computation.25 | convolution fusion | flops 205651968 | bytes 8155136 | tf_op jit(solution)/shard_map/bjgtl,bljd->bjgtd/dot_general | solution.py:107
  60.4 3.4 %concatenate.28 = bf16[64,1,2,28,128]{4,3,2,0,1:T(8,128)(2,1)S(1)} concatenate(bf16[64,1,2,24,128]{4,3,2,0,1:T(8,128)(2,1)} %fusion.18, bf16[64,1,2,1,128]{4,3,2,0,1:T(2,128)(2,1)S(1)} %copy.169, bf16[64,1,2,1,128]{4,3,2,0,1:T(2,128)(2,1)S(1)} %copy.170, bf16[64,1,2,1,128]{4,3,2,0,1:T(2,128)(2,1)S(1)} %copy.171, bf16[64,1,2,1,128]{4,3,2,0,1:T(2,128)(2,1)S(1)} %copy.172), dimensions={3} | concatenate | bytes 1835008 | tf_op jit(solution)/shard_map/concatenate | solution.py:119
  63.9 1.6 copy.173
  65.5 6.2 %all-to-all-start.1 = ((bf16[64,1,2,28,128]{4,2,3,1,0:T(2,128)(2,1)}), bf16[64,1,2,28,128]{4,2,3,1,0:T(2,128)(2,1)S(1)}, u32[]{:S(2)}, u32[]{:S(2)}) async-start(bf16[64,1,2,28,128]{4,2,3,1,0:T(2,128)(2,1)} %copy.173), calls=%async_computation.1 | async-start | bytes 1835008 | tf_op jit(solution)/shard_map/all_to_all | solution.py:124
  72.1 25.4 %all-to-all-done.1 = bf16[64,1,2,28,128]{4,2,3,1,0:T(2,128)(2,1)S(1)} async-done(((bf16[64,1,2,28,128]{4,2,3,1,0:T(2,128)(2,1)}), bf16[64,1,2,28,128]{4,2,3,1,0:T(2,128)(2,1)S(1)}, u32[]{:S(2)}, u32[]{:S(2)}) %all-to-all-start.1) | async-done | bytes 917536 | tf_op jit(solution)/shard_map/all_to_all | solution.py:124
  97.5 0.6 convert_element_type.44
  98.3 1.1 copy-done.2
  99.8 3.5 %fusion.7 = f32[2,24,128]{2,0,1:T(2,128)S(1)} fusion(f32[64,1,2,28,128]{4,2,3,1,0:T(2,128)} %copy-done.2, f32[64,2,24]{1,2,0:T(8,128)S(1)} %copy.176), kind=kLoop, calls=%fused_computation.13 | loop fusion | flops 780288 | bytes 1609728 | tf_op jit(solution)/shard_map/reduce_sum | solution.py:136
  103.6 1.5 fusion.44
  105.0 0.8 reshape.417
  105.8 6.8 %all-to-all-start.2 = ((f32[8,3,2048]{2,1,0:T(4,128)}), f32[8,3,2048]{2,1,0:T(4,128)S(1)}, u32[]{:S(2)}, u32[]{:S(2)}) async-start(f32[8,3,2048]{2,1,0:T(4,128)} %reshape.417), calls=%async_computation.2 | async-start | bytes 524288 | tf_op jit(solution)/shard_map/all_to_all | solution.py:147
  112.9 11.5 %all-to-all-done.2 = f32[8,3,2048]{2,1,0:T(4,128)S(1)} async-done(((f32[8,3,2048]{2,1,0:T(4,128)}), f32[8,3,2048]{2,1,0:T(4,128)S(1)}, u32[]{:S(2)}, u32[]{:S(2)}) %all-to-all-start.2) | async-done | bytes 196640 | tf_op jit(solution)/shard_map/all_to_all | solution.py:147
  124.4 1.0 multiply_reduce_fusion.1
  125.5 10.1 %all_to_all.30 = bf16[8,3,2048]{2,1,0:T(4,128)(2,1)S(1)} all-to-all(bf16[8,3,2048]{2,1,0:T(4,128)(2,1)S(1)} %broadcast_in_dim.122), channel_id=1, replica_groups=mesh['req'=64,'mdl'=8] {'mdl'}, dimensions={0} | all-to-all | bytes 196608 | tf_op jit(solution)/shard_map/all_to_all | solution.py:162
  135.6 0.7 reshape.418
  136.4 81.0 %all-gather.2.cloned.1.call-done = bf16[1536,2048]{1,0:T(8,128)(2,1)} async-done(((bf16[24,2048]{1,0:T(8,128)(2,1)}), bf16[1536,2048]{1,0:T(8,128)(2,1)}) %all-gather.2.cloned.1.call-update) | async-done | bytes 6291472 | tf_op jit(solution)/shard_map/all_gather | solution.py:166
  217.4 6.0 %fusion.67 = (f32[1536]{0:T(1024)S(1)}, f32[1536,256]{0,1:T(8,128)}) fusion(bf16[1536,2048]{1,0:T(8,128)(2,1)} %all-gather.2.cloned.1.call-done, bf16[2048,256]{1,0:T(8,128)(2,1)} %param.26), kind=kOutput, calls=%fused_computation.138 | convolution fusion | flops 1611004416 | bytes 8919040 | tf_op jit(solution)/shard_map/dot_general | solution.py:165
  223.5 1.9 fusion.8
  225.8 16.0 %all_to_all.31 = f32[64,24,4]{1,2,0:T(4,128)S(1)} all-to-all(f32[64,24,4]{1,2,0:T(4,128)S(1)} %copy.180), channel_id=1, replica_groups=mesh['req'=64,'mdl'=8] {'req'}, dimensions={0} | all-to-all | bytes 49152 | tf_op jit(solution)/shard_map/all_to_all | solution.py:186
  242.4 12.9 %all_to_all.32 = f32[8,24,4]{1,2,0:T(4,128)S(1)} all-to-all(f32[8,24,4]{1,2,0:T(4,128)S(1)} %broadcast_in_dim.124), channel_id=1, replica_groups=mesh['req'=64,'mdl'=8] {'mdl'}, dimensions={0} | all-to-all | bytes 6144 | tf_op jit(solution)/shard_map/all_to_all | solution.py:189
  (79 shorter events, 5.8 us)
Async XLA Ops:
  7.2 21.2 %copy-start = (bf16[2,34,128,128]{3,2,1,0:T(8,128)(2,1)S(1)}, bf16[2,34,128,128]{3,2,1,0:T(8,128)(2,1)}, u32[]{:S(2)}) copy-start(bf16[2,34,128,128]{3,2,1,0:T(8,128)(2,1)} %param.18) | copy-start | bytes 6684676
  9.0 37.8 %all-to-all-start = ((bf16[64,24,1,2,128]{4,1,3,2,0:T(8,128)(2,1)}), bf16[64,24,1,2,128]{4,1,3,2,0:T(8,128)(2,1)S(1)}, u32[]{:S(2)}, u32[]{:S(2)}) async-start(bf16[64,24,1,2,128]{4,1,3,2,0:T(8,128)(2,1)} %broadcast_in_dim.117), calls=%async_computation | async-start | bytes 1572864 | tf_op jit(solution)/shard_map/all_to_all | solution.py:70
  51.7 1.7 copy-start.1
  60.3 11.4 %copy-start.7 = (s32[1,24]{1,0:T(1,128)S(1)}, s32[1,24]{1,0:T(1,128)}, u32[]{:S(2)}) copy-start(s32[1,24]{1,0:T(1,128)} %param.22) | copy-start | bytes 292
  60.3 11.5 %copy-start.4 = (bf16[24,256]{1,0:T(8,128)(2,1)S(1)}, bf16[24,256]{1,0:T(8,128)(2,1)}, u32[]{:S(2)}) copy-start(bf16[24,256]{1,0:T(8,128)(2,1)} %param.15) | copy-start | bytes 36868
  63.9 8.0 %copy-start.8 = (bf16[2,24,128]{2,1,0:T(8,128)(2,1)S(1)}, bf16[2,24,128]{2,1,0:T(8,128)(2,1)}, u32[]{:S(2)}) copy-start(bf16[2,24,128]{2,1,0:T(8,128)(2,1)} %param.16) | copy-start | bytes 36868
  65.5 31.9 %all-to-all-start.1 = ((bf16[64,1,2,28,128]{4,2,3,1,0:T(2,128)(2,1)}), bf16[64,1,2,28,128]{4,2,3,1,0:T(2,128)(2,1)S(1)}, u32[]{:S(2)}, u32[]{:S(2)}) async-start(bf16[64,1,2,28,128]{4,2,3,1,0:T(2,128)(2,1)} %copy.173), calls=%async_computation.1 | async-start | bytes 1835008 | tf_op jit(solution)/shard_map/all_to_all | solution.py:124
  72.0 31.5 %copy-start.3 = (bf16[24,256]{1,0:T(8,128)(2,1)S(1)}, bf16[24,256]{1,0:T(8,128)(2,1)}, u32[]{:S(2)}) copy-start(bf16[24,256]{1,0:T(8,128)(2,1)} %param.17) | copy-start | bytes 36868
  98.1 1.3 copy-start.2
  98.1 14.8 %copy-start.6 = (bf16[2048]{0:T(1024)(128)(2,1)S(1)}, bf16[2048]{0:T(1024)(128)(2,1)}, u32[]{:S(2)}) copy-start(bf16[2048]{0:T(1024)(128)(2,1)} %param.25) | copy-start | bytes 12292
  105.8 18.5 %all-to-all-start.2 = ((f32[8,3,2048]{2,1,0:T(4,128)}), f32[8,3,2048]{2,1,0:T(4,128)S(1)}, u32[]{:S(2)}, u32[]{:S(2)}) async-start(f32[8,3,2048]{2,1,0:T(4,128)} %reshape.417), calls=%async_computation.2 | async-start | bytes 524288 | tf_op jit(solution)/shard_map/all_to_all | solution.py:147
  112.7 104.8 %all-gather.2.cloned.1.call-start = ((), (), s32[]{:S(2)}) async-start(), calls=%async_computation.6 | async-start | bytes 6389760 | tf_op jit(solution)/shard_map/all_gather | solution.py:166
  136.4 87.1 %copy-start.5 = (s32[1536]{0:T(1024)S(1)}, s32[1536]{0:T(1024)}, u32[]{:S(2)}) copy-start(s32[1536]{0:T(1024)} %param.27) | copy-start | bytes 18436
Sparse Core Ops, SparseCore 0:
  136.5 80.8 all-gather.1

commit v3 on v2

--- a/solution.py
+++ b/solution.py
@@ -87,29 +87,60 @@
     ]
     send_slot = jnp.take(jnp.stack(slot_picks, axis=1), holder, axis=0).reshape(-1)
     send_fill = jnp.take(jnp.stack(fill_picks, axis=1), holder, axis=0)
-    outgoing = jnp.take(page_kv, send_slot, axis=1, mode="clip").reshape(
-        2, groups, CAP * page_len, kv_heads, HEAD_SIZE
-    )
-    live_keys = (
-        jnp.arange(page_len, dtype=jnp.int32)[None, None, :] < send_fill[:, :, None]
-    ).reshape(groups, CAP * page_len)
-    scores = (
+    stored = req_index * store_pages + jnp.arange(store_pages, dtype=jnp.int32)
+    match = page_table[None, :, :] == stored[:, None, None]
+    slot_used = jnp.any(match, axis=(1, 2))
+    slot_request = jnp.sum(jnp.where(match, indices[None, :, None], 0), axis=(1, 2))
+    slot_position = jnp.sum(
+        jnp.where(match, jnp.arange(page_slots, dtype=jnp.int32)[None, None, :], 0), axis=(1, 2)
+    )
+    slot_fill = jnp.where(
+        slot_used,
+        jnp.clip(
+            jnp.take(lengths, slot_request, mode="clip") - slot_position * page_len, 0, page_len
+        ),
+        0,
+    )
+    slot_dest = jnp.take(assignment, slot_request, mode="clip")
+    slot_queries = jnp.take(all_queries, slot_dest, axis=0, mode="clip")
+    slot_keys = page_kv[0].reshape(store_pages, page_len, kv_heads, HEAD_SIZE)
+    slot_values = page_kv[1].reshape(store_pages, page_len, kv_heads, HEAD_SIZE)
+    slot_live = (jnp.arange(page_len, dtype=jnp.int32)[None, :] < slot_fill[:, None])[
+        :, None, None, None, :
+    ]
+    slot_scores = (
         jnp.einsum(
-            "btjgd,bljd->bjgtl", all_queries, outgoing[0], preferred_element_type=jnp.float32
+            "stjgd,sljd->sjgtl", slot_queries, slot_keys, preferred_element_type=jnp.float32
         )
         * score_scale
     )
-    live = live_keys[:, None, None, None, :]
-    scores = jnp.where(live, scores, FLOOR_SCORE)
-    part_top = lax.reduce_precision(jnp.max(scores, axis=-1), exponent_bits=8, mantissa_bits=7)
-    weights = jnp.where(live, jnp.exp(scores - part_top[..., None]), 0.0)
-    part_sum = jnp.sum(weights, axis=-1)
-    part_acc = jnp.einsum(
-        "bjgtl,bljd->bjgtd",
-        weights.astype(jnp.bfloat16),
-        outgoing[1],
+    slot_scores = jnp.where(slot_live, slot_scores, FLOOR_SCORE)
+    slot_top = lax.reduce_precision(
+        jnp.max(slot_scores, axis=-1), exponent_bits=8, mantissa_bits=7
+    )
+    slot_weights = jnp.where(slot_live, jnp.exp(slot_scores - slot_top[..., None]), 0.0)
+    slot_sum = jnp.sum(slot_weights, axis=-1)
+    slot_acc = jnp.einsum(
+        "sjgtl,sljd->sjgtd",
+        slot_weights.astype(jnp.bfloat16),
+        slot_values,
         preferred_element_type=jnp.float32,
     )
+    present = (send_fill > 0).reshape(-1)
+    bucket = (groups, CAP) + slot_top.shape[1:]
+    cap_top = jnp.where(
+        present[:, None, None, None], jnp.take(slot_top, send_slot, axis=0, mode="clip"), FLOOR_SCORE
+    ).reshape(bucket)
+    cap_sum = jnp.where(
+        present[:, None, None, None], jnp.take(slot_sum, send_slot, axis=0, mode="clip"), 0.0
+    ).reshape(bucket)
+    cap_acc = jnp.where(
+        present[:, None, None, None, None], jnp.take(slot_acc, send_slot, axis=0, mode="clip"), 0.0
+    ).reshape(bucket + (HEAD_SIZE,))
+    part_top = jnp.max(cap_top, axis=1)
+    cap_scale = jnp.exp(cap_top - part_top[:, None])
+    part_sum = jnp.sum(cap_sum * cap_scale, axis=1)
+    part_acc = jnp.sum(cap_acc * cap_scale[..., None], axis=1)
     sum_high = lax.reduce_precision(part_sum, exponent_bits=8, mantissa_bits=7)
     sum_rest = part_sum - sum_high
     sum_mid = lax.reduce_precision(sum_rest, exponent_bits=8, mantissa_bits=7)

time: 264 us -> 258 us (0.977)
  waiting for transfers between devices: 124 us -> 134 us
  matrix products: 17.8 us -> 7.85 us
  local copies, waits for them, and re-layouts: 26.8 us -> 18 us
    all_to_all x1, waiting for transfers between devices: 5.78 us -> 16.5 us  [body(): lax.all_to_all(jnp.broadcast_to(query_heads[None], (groups,) + query_head...]
    dot_general x2, matrix products: 9.97 us -> 2.61 us  [the longest x1 2.1 us: body(): jnp.einsum('stjgd,sljd->sjgtl', slot_queries, slot_keys, preferred_elemen...]
    slice x1 -> x0, local copies, waits for them, and re-layouts: 6.06 us -> none  [body(): outgoing[0]]
    reduce_sum x1 -> x4, other arithmetic: 1.42 us -> 5.12 us  [the longest x1 2.75 us: body(): part_acc = jnp.sum(cap_acc * cap_scale[..., None], axis=1)]
    gather x1 -> x6, local copies, waits for them, and re-layouts: 6.37 us -> 8.04 us  [the longest x1 2.51 us: body(): slot_queries = jnp.take(all_queries, slot_dest, axis=0, mode='clip')]
  transfers between devices with their start and end apart: 4 -> 4, of which waited for: 4 -> 4; matrix products, arithmetic and copies ran while one was open for 7% -> 3% of each run, Pallas kernels for 0% -> 0%
where the time goes in v3:
time: 258 us
  waiting for transfers between devices  134 us (52%)
  blocking collectives  39.1 us (15%)
  starting transfers between devices  28.2 us (11%)
  local copies, waits for them, and re-layouts  18 us (7%)
  other arithmetic  15.4 us (6%)
  between operations  14.6 us (6%)
  matrix products  7.85 us (3%)
    all_gather x1, waiting for transfers between devices, body(): lax.all_gather(normed, 'req', axis=0, tiled=True)  81 us
    all_to_all x1, waiting for transfers between devices, body(): lax.all_to_all(payload, 'req', 0, 0, tiled=True).astype(jnp.float32)  25.3 us
    all_to_all x1, waiting for transfers between devices, body(): lax.all_to_all(jnp.broadcast_to(query_heads[None], (groups,) + query_head...  16.5 us
    all_to_all x1, blocking collectives, body(): stats = lax.all_to_all(stats, 'req', 0, 0, tiled=True)  16 us
    all_to_all x1, starting transfers between devices, body(): lax.all_to_all(jnp.broadcast_to(query_heads[None], (groups,) + query_head...  15 us
    all_to_all x1, blocking collectives, body(): lax.all_to_all(jnp.broadcast_to(stats[None], (mdl_size,) + stats.shape),...  12.9 us
    all_to_all x1, waiting for transfers between devices, body(): lax.all_to_all(update.reshape(mdl_size, share, update.shape[1]), 'mdl', 0...  11.6 us
    all_to_all x1, blocking collectives, body(): lax.all_to_all(jnp.broadcast_to(normed_rows[None], (mdl_size,) + normed_r...  10.1 us
  transfers between devices with their start and end apart: 4, of which 4 were waited for; matrix products, arithmetic and copies ran while one was open for 3% of the time, Pallas kernels for 0%

profile of v3, /device:TPU:1, one launch (start us, length us, event | category | flops | bytes accessed | tf_op | source)
XLA Modules:
  0.0 257.7 jit_solution(3406022081674405252)
XLA Ops:
  7.2 0.8 copy_bitcast_fusion
  8.0 1.0 broadcast_in_dim.198
  9.0 15.0 %all-to-all-start = ((bf16[64,24,1,2,128]{4,1,3,2,0:T(8,128)(2,1)}), bf16[64,24,1,2,128]{4,1,3,2,0:T(8,128)(2,1)}, u32[]{:S(2)}, u32[]{:S(2)}) async-start(bf16[64,24,1,2,128]{4,1,3,2,0:T(8,128)(2,1)} %broadcast_in_dim.198), calls=%async_computation | async-start | bytes 1572864 | tf_op jit(solution)/shard_map/all_to_all | solution.py:70
  24.2 1.5 fusion.6
  25.7 0.8 gather_fusion.1
  26.5 0.8 gather_fusion
  29.4 0.8 compare_reduce_fusion
  30.4 16.5 %all-to-all-done = bf16[64,24,1,2,128]{4,1,3,2,0:T(8,128)(2,1)} async-done(((bf16[64,24,1,2,128]{4,1,3,2,0:T(8,128)(2,1)}), bf16[64,24,1,2,128]{4,1,3,2,0:T(8,128)(2,1)}, u32[]{:S(2)}, u32[]{:S(2)}) %all-to-all-start) | async-done | bytes 786464 | tf_op jit(solution)/shard_map/all_to_all | solution.py:70
  46.9 2.5 gather_fusion.2
  49.4 2.1 fusion.60
  51.5 0.6 fusion.17
  52.7 0.8 gather_fusion.4
  53.8 0.7 gather_fusion.5
  55.5 2.5 gather_fusion.3
  58.0 2.8 %multiply_reduce_fusion = bf16[64,2,24,128]{3,2,1,0:T(8,128)(2,1)S(1)} fusion(f32[64,2,1,2,24,128]{5,4,3,1,0,2:T(8,128)} %bitcast.159, f32[64,2,2,24]{3,2,1,0:T(2,128)S(1)} %subtract_exponential_fusion.1, pred[64,2]{1,0:T(8,128)(4,1)S(1)} %select_compare_fusion), kind=kLoop, calls=%fused_computation.8 | loop fusion | flops 1966080 | bytes 3956864 | tf_op jit(solution)/shard_map/reduce_sum | solution.py:143
  60.8 0.9 concatenate.28
  61.7 1.7 copy.216
  63.4 6.4 %all-to-all-start.1 = ((bf16[64,1,2,28,128]{4,2,3,1,0:T(2,128)(2,1)}), bf16[64,1,2,28,128]{4,2,3,1,0:T(2,128)(2,1)}, u32[]{:S(2)}, u32[]{:S(2)}) async-start(bf16[64,1,2,28,128]{4,2,3,1,0:T(2,128)(2,1)} %copy.216), calls=%async_computation.1 | async-start | bytes 1835008 | tf_op jit(solution)/shard_map/all_to_all | solution.py:155
  70.1 25.3 %all-to-all-done.1 = bf16[64,1,2,28,128]{4,2,3,1,0:T(2,128)(2,1)} async-done(((bf16[64,1,2,28,128]{4,2,3,1,0:T(2,128)(2,1)}), bf16[64,1,2,28,128]{4,2,3,1,0:T(2,128)(2,1)}, u32[]{:S(2)}, u32[]{:S(2)}) %all-to-all-start.1) | async-done | bytes 917536 | tf_op jit(solution)/shard_map/all_to_all | solution.py:155
  95.5 1.8 convert_element_type.44
  97.5 1.3 copy.219
  98.8 3.4 %fusion = f32[2,24,128]{2,0,1:T(2,128)S(1)} fusion(f32[64,1,2,28,128]{4,2,3,1,0:T(2,128)S(1)} %convert_element_type.44, f32[64,2,24]{1,2,0:T(8,128)} %copy.219), kind=kLoop, calls=%fused_computation.13 | loop fusion | flops 780288 | bytes 1609728 | tf_op jit(solution)/shard_map/reduce_sum | solution.py:167
  102.8 0.8 reshape.543
  103.6 6.8 %all-to-all-start.2 = ((f32[8,3,2048]{2,1,0:T(4,128)}), f32[8,3,2048]{2,1,0:T(4,128)S(1)}, u32[]{:S(2)}, u32[]{:S(2)}) async-start(f32[8,3,2048]{2,1,0:T(4,128)} %reshape.543), calls=%async_computation.2 | async-start | bytes 524288 | tf_op jit(solution)/shard_map/all_to_all | solution.py:178
  110.4 11.6 %all-to-all-done.2 = f32[8,3,2048]{2,1,0:T(4,128)S(1)} async-done(((f32[8,3,2048]{2,1,0:T(4,128)}), f32[8,3,2048]{2,1,0:T(4,128)S(1)}, u32[]{:S(2)}, u32[]{:S(2)}) %all-to-all-start.2) | async-done | bytes 196640 | tf_op jit(solution)/shard_map/all_to_all | solution.py:178
  122.1 1.0 multiply_reduce_fusion.3
  123.2 10.1 %all_to_all.30 = bf16[8,3,2048]{2,1,0:T(4,128)(2,1)S(1)} all-to-all(bf16[8,3,2048]{2,1,0:T(4,128)(2,1)S(1)} %broadcast_in_dim.211), channel_id=1, replica_groups=mesh['req'=64,'mdl'=8] {'mdl'}, dimensions={0} | all-to-all | bytes 196608 | tf_op jit(solution)/shard_map/all_to_all | solution.py:193
  133.4 0.7 reshape.544
  134.1 81.0 %all-gather.2.cloned.1.call-done = bf16[1536,2048]{1,0:T(8,128)(2,1)} async-done(((bf16[24,2048]{1,0:T(8,128)(2,1)}), bf16[1536,2048]{1,0:T(8,128)(2,1)}) %all-gather.2.cloned.1.call-update) | async-done | bytes 6291472 | tf_op jit(solution)/shard_map/all_gather | solution.py:197
  215.1 4.6 %fusion.62 = (f32[1536]{0:T(1024)S(1)}, f32[1536,256]{0,1:T(8,128)S(1)}) fusion(bf16[1536,2048]{1,0:T(8,128)(2,1)} %all-gather.2.cloned.1.call-done, bf16[2048,256]{1,0:T(8,128)(2,1)S(1)} %copy-done), kind=kOutput, calls=%fused_computation.152 | convolution fusion | flops 1611004416 | bytes 8919040 | tf_op jit(solution)/shard_map/dot_general | solution.py:196
  220.7 16.0 %all_to_all.31 = f32[64,24,4]{1,2,0:T(4,128)S(1)} all-to-all(f32[64,24,4]{1,2,0:T(4,128)S(1)} %copy.223), channel_id=1, replica_groups=mesh['req'=64,'mdl'=8] {'req'}, dimensions={0} | all-to-all | bytes 49152 | tf_op jit(solution)/shard_map/all_to_all | solution.py:217
  237.4 12.9 %all_to_all.32 = f32[8,24,4]{1,2,0:T(4,128)S(1)} all-to-all(f32[8,24,4]{1,2,0:T(4,128)S(1)} %broadcast_in_dim.213), channel_id=1, replica_groups=mesh['req'=64,'mdl'=8] {'mdl'}, dimensions={0} | all-to-all | bytes 6144 | tf_op jit(solution)/shard_map/all_to_all | solution.py:220
  (101 shorter events, 7.6 us)
Async XLA Ops:
  7.2 208.0 %copy-start = (bf16[2048,256]{1,0:T(8,128)(2,1)S(1)}, bf16[2048,256]{1,0:T(8,128)(2,1)}, u32[]{:S(2)}) copy-start(bf16[2048,256]{1,0:T(8,128)(2,1)} %param.26) | copy-start | bytes 3145732
  7.2 16.9 %copy-start.2 = (s32[64]{0:T(128)S(1)}, s32[64]{0:T(128)}, u32[]{:S(2)}) copy-start(s32[64]{0:T(128)} %param.21) | copy-start | bytes 772
  7.2 17.0 %copy-start.6 = (s32[64,128]{1,0:T(8,128)S(1)}, s32[64,128]{1,0:T(8,128)}, u32[]{:S(2)}) copy-start(s32[64,128]{1,0:T(8,128)} %param.19) | copy-start | bytes 98308
  7.2 19.3 %copy-start.1 = (s32[64]{0:T(128)S(1)}, s32[64]{0:T(128)}, u32[]{:S(2)}) copy-start(s32[64]{0:T(128)} %param.20) | copy-start | bytes 772
  9.0 37.9 %all-to-all-start = ((bf16[64,24,1,2,128]{4,1,3,2,0:T(8,128)(2,1)}), bf16[64,24,1,2,128]{4,1,3,2,0:T(8,128)(2,1)}, u32[]{:S(2)}, u32[]{:S(2)}) async-start(bf16[64,24,1,2,128]{4,1,3,2,0:T(8,128)(2,1)} %broadcast_in_dim.198), calls=%async_computation | async-start | bytes 1572864 | tf_op jit(solution)/shard_map/all_to_all | solution.py:70
  24.0 25.4 %copy-start.3 = (bf16[2,34,128,128]{3,2,1,0:T(8,128)(2,1)S(1)}, bf16[2,34,128,128]{3,2,1,0:T(8,128)(2,1)}, u32[]{:S(2)}) copy-start(bf16[2,34,128,128]{3,2,1,0:T(8,128)(2,1)} %param.18) | copy-start | bytes 6684676
  49.4 2.7 %copy-start.4 = (bf16[2,34,128,128]{3,2,1,0:T(8,128)(2,1)S(1)}, bf16[2,34,128,128]{3,2,1,0:T(8,128)(2,1)}, u32[]{:S(2)}) copy-start(bf16[2,34,128,128]{3,2,1,0:T(8,128)(2,1)} %param.18) | copy-start | bytes 6684676
  61.7 8.1 %copy-start.11 = (s32[1,24]{1,0:T(1,128)S(1)}, s32[1,24]{1,0:T(1,128)}, u32[]{:S(2)}) copy-start(s32[1,24]{1,0:T(1,128)} %param.22) | copy-start | bytes 292
  61.7 8.2 %copy-start.8 = (bf16[24,256]{1,0:T(8,128)(2,1)S(1)}, bf16[24,256]{1,0:T(8,128)(2,1)}, u32[]{:S(2)}) copy-start(bf16[24,256]{1,0:T(8,128)(2,1)} %param.15) | copy-start | bytes 36868
  61.7 8.2 %copy-start.12 = (bf16[2,24,128]{2,1,0:T(8,128)(2,1)S(1)}, bf16[2,24,128]{2,1,0:T(8,128)(2,1)}, u32[]{:S(2)}) copy-start(bf16[2,24,128]{2,1,0:T(8,128)(2,1)} %param.16) | copy-start | bytes 36868
  63.4 32.0 %all-to-all-start.1 = ((bf16[64,1,2,28,128]{4,2,3,1,0:T(2,128)(2,1)}), bf16[64,1,2,28,128]{4,2,3,1,0:T(2,128)(2,1)}, u32[]{:S(2)}, u32[]{:S(2)}) async-start(bf16[64,1,2,28,128]{4,2,3,1,0:T(2,128)(2,1)} %copy.216), calls=%async_computation.1 | async-start | bytes 1835008 | tf_op jit(solution)/shard_map/all_to_all | solution.py:155
  97.5 5.0 %copy-start.7 = (bf16[24,256]{1,0:T(8,128)(2,1)S(1)}, bf16[24,256]{1,0:T(8,128)(2,1)}, u32[]{:S(2)}) copy-start(bf16[24,256]{1,0:T(8,128)(2,1)} %param.17) | copy-start | bytes 36868
  98.8 3.7 %copy-start.5 = (bf16[256,2048]{1,0:T(8,128)(2,1)S(1)}, bf16[256,2048]{1,0:T(8,128)(2,1)}, u32[]{:S(2)}) copy-start(bf16[256,2048]{1,0:T(8,128)(2,1)} %param.24) | copy-start | bytes 3145732
  102.3 8.2 %copy-start.10 = (bf16[2048]{0:T(1024)(128)(2,1)S(1)}, bf16[2048]{0:T(1024)(128)(2,1)}, u32[]{:S(2)}) copy-start(bf16[2048]{0:T(1024)(128)(2,1)} %param.25) | copy-start | bytes 12292
  103.6 18.5 %all-to-all-start.2 = ((f32[8,3,2048]{2,1,0:T(4,128)}), f32[8,3,2048]{2,1,0:T(4,128)S(1)}, u32[]{:S(2)}, u32[]{:S(2)}) async-start(f32[8,3,2048]{2,1,0:T(4,128)} %reshape.543), calls=%async_computation.2 | async-start | bytes 524288 | tf_op jit(solution)/shard_map/all_to_all | solution.py:178
  110.4 104.8 %all-gather.2.cloned.1.call-start = ((), (), s32[]{:S(2)}) async-start(), calls=%async_computation.6 | async-start | bytes 6389760 | tf_op jit(solution)/shard_map/all_gather | solution.py:197
  134.1 85.7 %copy-start.9 = (s32[1536]{0:T(1024)S(1)}, s32[1536]{0:T(1024)}, u32[]{:S(2)}) copy-start(s32[1536]{0:T(1024)} %param.27) | copy-start | bytes 18436
Sparse Core Ops, SparseCore 0:
  134.2 80.8 all-gather.1

commit v4 on v3

--- a/solution.py
+++ b/solution.py
@@ -152,13 +152,11 @@
         + [jnp.pad(v, pad)[..., None, :] for v in (part_top, sum_high, sum_mid, sum_low)],
         axis=3,
     ).astype(jnp.bfloat16)
-    arrived = lax.all_to_all(payload, "req", 0, 0, tiled=True).astype(jnp.float32)
-    arrived_acc = arrived[:, :, :, :fresh_count, :]
-    arrived_top = arrived[:, :, :, fresh_count, :fresh_count]
-    arrived_sum = (
-        arrived[:, :, :, fresh_count + 1, :fresh_count]
-        + arrived[:, :, :, fresh_count + 2, :fresh_count]
-    ) + arrived[:, :, :, fresh_count + 3, :fresh_count]
+    arrived = lax.all_to_all(payload, "req", 0, 0, tiled=True)
+    arrived_acc = arrived[:, :, :, :fresh_count, :].astype(jnp.float32)
+    arrived_rows = arrived[:, :, :, fresh_count:, :fresh_count].astype(jnp.float32)
+    arrived_top = arrived_rows[:, :, :, 0]
+    arrived_sum = (arrived_rows[:, :, :, 1] + arrived_rows[:, :, :, 2]) + arrived_rows[:, :, :, 3]
     row_top = jnp.maximum(jnp.max(arrived_top, axis=0), fresh_top)
     arrived_scale = jnp.exp(arrived_top - row_top[None])
     fresh_scale = jnp.exp(fresh_top - row_top)

time: 258 us -> 254 us (0.984)
  other arithmetic: 15.4 us -> 12.2 us
where the time goes in v4:
time: 254 us; the launch traced here: 253 us
  waiting for transfers between devices  135 us (53%)
  blocking collectives  39.1 us (15%)
  starting transfers between devices  28.1 us (11%)
  local copies, waits for them, and re-layouts  17.1 us (7%)
  between operations  14.6 us (6%)
  other arithmetic  12.2 us (5%)
  matrix products  7.85 us (3%)
    all_gather x1, waiting for transfers between devices, body(): lax.all_gather(normed, 'req', axis=0, tiled=True)  81 us
    all_to_all x1, waiting for transfers between devices, body(): arrived = lax.all_to_all(payload, 'req', 0, 0, tiled=True)  25.4 us
    all_to_all x1, waiting for transfers between devices, body(): lax.all_to_all(jnp.broadcast_to(query_heads[None], (groups,) + query_head...  16.5 us
    all_to_all x1, blocking collectives, body(): stats = lax.all_to_all(stats, 'req', 0, 0, tiled=True)  16 us
    all_to_all x1, starting transfers between devices, body(): lax.all_to_all(jnp.broadcast_to(query_heads[None], (groups,) + query_head...  15 us
    all_to_all x1, blocking collectives, body(): lax.all_to_all(jnp.broadcast_to(stats[None], (mdl_size,) + stats.shape),...  12.9 us
    all_to_all x1, waiting for transfers between devices, body(): lax.all_to_all(update.reshape(mdl_size, share, update.shape[1]), 'mdl', 0...  11.6 us
    all_to_all x1, blocking collectives, body(): lax.all_to_all(jnp.broadcast_to(normed_rows[None], (mdl_size,) + normed_r...  10.1 us
  transfers between devices with their start and end apart: 4, of which 4 were waited for; matrix products, arithmetic and copies ran while one was open for 3% of the time, Pallas kernels for 0%

profile of v4, /device:TPU:1, one launch (start us, length us, event | category | flops | bytes accessed | tf_op | source)
XLA Modules:
  0.0 253.5 jit_solution(18412985080879570330)
XLA Ops:
  7.2 0.8 copy_bitcast_fusion
  8.0 1.0 broadcast_in_dim.198
  9.0 15.0 %all-to-all-start = ((bf16[64,24,1,2,128]{4,1,3,2,0:T(8,128)(2,1)}), bf16[64,24,1,2,128]{4,1,3,2,0:T(8,128)(2,1)}, u32[]{:S(2)}, u32[]{:S(2)}) async-start(bf16[64,24,1,2,128]{4,1,3,2,0:T(8,128)(2,1)} %broadcast_in_dim.198), calls=%async_computation | async-start | bytes 1572864 | tf_op jit(solution)/shard_map/all_to_all | solution.py:70
  24.2 1.5 fusion.5
  25.7 0.8 gather_fusion.1
  26.5 0.8 gather_fusion
  28.0 0.6 gather_fusion.6
  28.6 0.6 gather_fusion.7
  29.4 0.8 compare_reduce_fusion
  30.4 16.5 %all-to-all-done = bf16[64,24,1,2,128]{4,1,3,2,0:T(8,128)(2,1)} async-done(((bf16[64,24,1,2,128]{4,1,3,2,0:T(8,128)(2,1)}), bf16[64,24,1,2,128]{4,1,3,2,0:T(8,128)(2,1)}, u32[]{:S(2)}, u32[]{:S(2)}) %all-to-all-start) | async-done | bytes 786464 | tf_op jit(solution)/shard_map/all_to_all | solution.py:70
  46.9 2.5 gather_fusion.2
  49.4 2.1 fusion.59
  51.5 0.6 fusion.16
  52.7 0.8 gather_fusion.4
  53.8 0.7 gather_fusion.5
  55.5 2.5 gather_fusion.3
  58.0 2.8 %multiply_reduce_fusion = bf16[64,2,24,128]{3,2,1,0:T(8,128)(2,1)S(1)} fusion(f32[64,2,1,2,24,128]{5,4,3,1,0,2:T(8,128)} %bitcast.159, f32[64,2,2,24]{3,2,1,0:T(2,128)S(1)} %subtract_exponential_fusion.1, pred[64,2]{1,0:T(8,128)(4,1)S(1)} %select_compare_fusion), kind=kLoop, calls=%fused_computation.8 | loop fusion | flops 1966080 | bytes 3956864 | tf_op jit(solution)/shard_map/reduce_sum | solution.py:143
  60.8 0.9 concatenate.28
  61.7 1.6 copy.216
  63.4 6.2 %all-to-all-start.1 = ((bf16[64,1,2,28,128]{4,2,3,1,0:T(2,128)(2,1)}), bf16[64,1,2,28,128]{4,2,3,1,0:T(2,128)(2,1)S(1)}, u32[]{:S(2)}, u32[]{:S(2)}) async-start(bf16[64,1,2,28,128]{4,2,3,1,0:T(2,128)(2,1)} %copy.216), calls=%async_computation.1 | async-start | bytes 1835008 | tf_op jit(solution)/shard_map/all_to_all | solution.py:155
  69.9 25.4 %all-to-all-done.1 = bf16[64,1,2,28,128]{4,2,3,1,0:T(2,128)(2,1)S(1)} async-done(((bf16[64,1,2,28,128]{4,2,3,1,0:T(2,128)(2,1)}), bf16[64,1,2,28,128]{4,2,3,1,0:T(2,128)(2,1)S(1)}, u32[]{:S(2)}, u32[]{:S(2)}) %all-to-all-start.1) | async-done | bytes 917536 | tf_op jit(solution)/shard_map/all_to_all | solution.py:155
  96.1 1.9 multiply_reduce_fusion.2
  98.6 0.8 reshape.543
  99.3 6.8 %all-to-all-start.2 = ((f32[8,3,2048]{2,1,0:T(4,128)}), f32[8,3,2048]{2,1,0:T(4,128)S(1)}, u32[]{:S(2)}, u32[]{:S(2)}) async-start(f32[8,3,2048]{2,1,0:T(4,128)} %reshape.543), calls=%async_computation.2 | async-start | bytes 524288 | tf_op jit(solution)/shard_map/all_to_all | solution.py:176
  106.2 11.6 %all-to-all-done.2 = f32[8,3,2048]{2,1,0:T(4,128)S(1)} async-done(((f32[8,3,2048]{2,1,0:T(4,128)}), f32[8,3,2048]{2,1,0:T(4,128)S(1)}, u32[]{:S(2)}, u32[]{:S(2)}) %all-to-all-start.2) | async-done | bytes 196640 | tf_op jit(solution)/shard_map/all_to_all | solution.py:176
  117.9 1.0 multiply_reduce_fusion.4
  119.0 10.1 %all_to_all.30 = bf16[8,3,2048]{2,1,0:T(4,128)(2,1)S(1)} all-to-all(bf16[8,3,2048]{2,1,0:T(4,128)(2,1)S(1)} %broadcast_in_dim.211), channel_id=1, replica_groups=mesh['req'=64,'mdl'=8] {'mdl'}, dimensions={0} | all-to-all | bytes 196608 | tf_op jit(solution)/shard_map/all_to_all | solution.py:191
  129.2 0.7 reshape.544
  129.9 81.0 %all-gather.2.cloned.1.call-done = bf16[1536,2048]{1,0:T(8,128)(2,1)} async-done(((bf16[24,2048]{1,0:T(8,128)(2,1)}), bf16[1536,2048]{1,0:T(8,128)(2,1)}) %all-gather.2.cloned.1.call-update) | async-done | bytes 6291472 | tf_op jit(solution)/shard_map/all_gather | solution.py:195
  210.9 4.6 %fusion.61 = (f32[1536]{0:T(1024)S(1)}, f32[1536,256]{0,1:T(8,128)S(1)}) fusion(bf16[1536,2048]{1,0:T(8,128)(2,1)} %all-gather.2.cloned.1.call-done, bf16[2048,256]{1,0:T(8,128)(2,1)S(1)} %copy-done), kind=kOutput, calls=%fused_computation.152 | convolution fusion | flops 1611004416 | bytes 8919040 | tf_op jit(solution)/shard_map/dot_general | solution.py:194
  216.5 16.0 %all_to_all.31 = f32[64,24,4]{1,2,0:T(4,128)S(1)} all-to-all(f32[64,24,4]{1,2,0:T(4,128)S(1)} %copy.223), channel_id=1, replica_groups=mesh['req'=64,'mdl'=8] {'req'}, dimensions={0} | all-to-all | bytes 49152 | tf_op jit(solution)/shard_map/all_to_all | solution.py:215
  233.1 12.9 %all_to_all.32 = f32[8,24,4]{1,2,0:T(4,128)S(1)} all-to-all(f32[8,24,4]{1,2,0:T(4,128)S(1)} %broadcast_in_dim.213), channel_id=1, replica_groups=mesh['req'=64,'mdl'=8] {'mdl'}, dimensions={0} | all-to-all | bytes 6144 | tf_op jit(solution)/shard_map/all_to_all | solution.py:218
  (101 shorter events, 6.9 us)
Async XLA Ops:
  7.2 203.8 %copy-start = (bf16[2048,256]{1,0:T(8,128)(2,1)S(1)}, bf16[2048,256]{1,0:T(8,128)(2,1)}, u32[]{:S(2)}) copy-start(bf16[2048,256]{1,0:T(8,128)(2,1)} %param.26) | copy-start | bytes 3145732
  7.2 16.9 %copy-start.2 = (s32[64]{0:T(128)S(1)}, s32[64]{0:T(128)}, u32[]{:S(2)}) copy-start(s32[64]{0:T(128)} %param.21) | copy-start | bytes 772
  7.2 17.0 %copy-start.6 = (s32[64,128]{1,0:T(8,128)S(1)}, s32[64,128]{1,0:T(8,128)}, u32[]{:S(2)}) copy-start(s32[64,128]{1,0:T(8,128)} %param.19) | copy-start | bytes 98308
  7.2 19.3 %copy-start.1 = (s32[64]{0:T(128)S(1)}, s32[64]{0:T(128)}, u32[]{:S(2)}) copy-start(s32[64]{0:T(128)} %param.20) | copy-start | bytes 772
  9.0 37.9 %all-to-all-start = ((bf16[64,24,1,2,128]{4,1,3,2,0:T(8,128)(2,1)}), bf16[64,24,1,2,128]{4,1,3,2,0:T(8,128)(2,1)}, u32[]{:S(2)}, u32[]{:S(2)}) async-start(bf16[64,24,1,2,128]{4,1,3,2,0:T(8,128)(2,1)} %broadcast_in_dim.198), calls=%async_computation | async-start | bytes 1572864 | tf_op jit(solution)/shard_map/all_to_all | solution.py:70
  24.0 25.4 %copy-start.3 = (bf16[2,34,128,128]{3,2,1,0:T(8,128)(2,1)S(1)}, bf16[2,34,128,128]{3,2,1,0:T(8,128)(2,1)}, u32[]{:S(2)}) copy-start(bf16[2,34,128,128]{3,2,1,0:T(8,128)(2,1)} %param.18) | copy-start | bytes 6684676
  49.4 2.7 %copy-start.4 = (bf16[2,34,128,128]{3,2,1,0:T(8,128)(2,1)S(1)}, bf16[2,34,128,128]{3,2,1,0:T(8,128)(2,1)}, u32[]{:S(2)}) copy-start(bf16[2,34,128,128]{3,2,1,0:T(8,128)(2,1)} %param.18) | copy-start | bytes 6684676
  61.7 7.9 %copy-start.11 = (s32[1,24]{1,0:T(1,128)S(1)}, s32[1,24]{1,0:T(1,128)}, u32[]{:S(2)}) copy-start(s32[1,24]{1,0:T(1,128)} %param.22) | copy-start | bytes 292
  61.7 8.0 %copy-start.8 = (bf16[24,256]{1,0:T(8,128)(2,1)S(1)}, bf16[24,256]{1,0:T(8,128)(2,1)}, u32[]{:S(2)}) copy-start(bf16[24,256]{1,0:T(8,128)(2,1)} %param.15) | copy-start | bytes 36868
  61.7 8.0 %copy-start.12 = (bf16[2,24,128]{2,1,0:T(8,128)(2,1)S(1)}, bf16[2,24,128]{2,1,0:T(8,128)(2,1)}, u32[]{:S(2)}) copy-start(bf16[2,24,128]{2,1,0:T(8,128)(2,1)} %param.16) | copy-start | bytes 36868
  63.4 31.9 %all-to-all-start.1 = ((bf16[64,1,2,28,128]{4,2,3,1,0:T(2,128)(2,1)}), bf16[64,1,2,28,128]{4,2,3,1,0:T(2,128)(2,1)S(1)}, u32[]{:S(2)}, u32[]{:S(2)}) async-start(bf16[64,1,2,28,128]{4,2,3,1,0:T(2,128)(2,1)} %copy.216), calls=%async_computation.1 | async-start | bytes 1835008 | tf_op jit(solution)/shard_map/all_to_all | solution.py:155
  95.4 2.9 %copy-start.7 = (bf16[24,256]{1,0:T(8,128)(2,1)S(1)}, bf16[24,256]{1,0:T(8,128)(2,1)}, u32[]{:S(2)}) copy-start(bf16[24,256]{1,0:T(8,128)(2,1)} %param.17) | copy-start | bytes 36868
  96.1 2.2 copy-start.5
  98.1 8.2 %copy-start.10 = (bf16[2048]{0:T(1024)(128)(2,1)S(1)}, bf16[2048]{0:T(1024)(128)(2,1)}, u32[]{:S(2)}) copy-start(bf16[2048]{0:T(1024)(128)(2,1)} %param.25) | copy-start | bytes 12292
  99.3 18.5 %all-to-all-start.2 = ((f32[8,3,2048]{2,1,0:T(4,128)}), f32[8,3,2048]{2,1,0:T(4,128)S(1)}, u32[]{:S(2)}, u32[]{:S(2)}) async-start(f32[8,3,2048]{2,1,0:T(4,128)} %reshape.543), calls=%async_computation.2 | async-start | bytes 524288 | tf_op jit(solution)/shard_map/all_to_all | solution.py:176
  106.2 104.8 %all-gather.2.cloned.1.call-start = ((), (), s32[]{:S(2)}) async-start(), calls=%async_computation.6 | async-start | bytes 6389760 | tf_op jit(solution)/shard_map/all_gather | solution.py:195
  129.9 85.7 %copy-start.9 = (s32[1536]{0:T(1024)S(1)}, s32[1536]{0:T(1024)}, u32[]{:S(2)}) copy-start(s32[1536]{0:T(1024)} %param.27) | copy-start | bytes 18436
Sparse Core Ops, SparseCore 0:
  130.0 80.8 all-gather.1
